TPU v7x, 32 devices: a whole 2x2x4 slice. The times are simulated.
32 devices in a mesh: groups: 2 (over y), tensor: 4 (over z), seq: 2 (over x), load: 2 (over core).
Axes of the slice: x: 2, y: 2, z: 4, core: 2. Of those that a mesh axis runs over, the one named last changes fastest.
Arguments:
- tokens: bfloat16 [1024, 16384], P(('groups', 'tensor'), ('seq', 'load')), parts along dimension 0, may hold values from -21 to 21
- weight_query: bfloat16 [16384, 16384], P(('seq', 'load'), 'tensor'), may hold values from -0.046875 to 0.046875
- weight_keyval: bfloat16 [16384, 2048], P(('seq', 'load'), 'tensor'), may hold values from -0.046875 to 0.046875
- down_query: bfloat16 [16384, 1024], P(('seq', 'load'), ('groups', 'tensor')), parts along dimension 1, may hold values from -0.046875 to 0.046875
- down_keyval: bfloat16 [16384, 1024], P(('seq', 'load'), ('groups', 'tensor')), parts along dimension 1, may hold values from -0.046875 to 0.046875
- up_query: bfloat16 [1024, 16384], P(('groups', 'load'), 'tensor'), parts along dimension 0, may hold values from -0.5 to 0.5
- up_keyval: bfloat16 [1024, 2048], P(('groups', 'load'), 'tensor'), parts along dimension 0, may hold values from -0.5 to 0.5
- adapter_rank: int32 [8], P('groups'), parts along dimension 0, may hold values from 8 to 128, as said below
- token_lengths: int32 [8], P('groups'), parts along dimension 0, may hold values from 1 to 384, 512 in all
- adapter_slot: int32 [8], P('groups'), parts along dimension 0, may hold values from 0 to 3, each once
Outputs:
- context: bfloat16 [1024, 16384], P(('groups', 'seq', 'load'), 'tensor'), parts along dimension 0
- kv_cache: bfloat16 [1024, 2048], P(('groups', 'seq', 'load'), 'tensor'), parts along dimension 0
There are 2 independent parts, one for each index of `groups`. A program takes and returns all parts, laid end to end along the dimension named above; an argument that names none is the same for every part. Nothing has to cross between parts.
Inputs may be any that keep to these rules, and one draw needn't show every extreme that they name: `adapter_rank`: each rank is a power of two; some tenant has rank 128 and some has rank 8. `token_lengths`: the lengths sum to 512; some tenant has exactly 384 tokens. `adapter_slot`: each slot belongs to exactly one tenant.
All inputs are finite; a program needn't handle non-finite values.
Results may differ from a plain program's by a relative error of at most 0.0025.
The roundings to bfloat16 on the way count: a program that leaves them out, or rounds other values in their place, can miss the bound.
Values may be sent and summed in bfloat16 or wider, within the bound.
No kernel may reach another device: no remote copies, remote signals or barrier semaphores. Data moves between devices by JAX's collectives and lax.ppermute only.
A program may use at most 128 MiB of HBM per device.

v0:
```python
import math
import jax
import jax.numpy as jnp
from jax import lax
from jax.sharding import PartitionSpec as P

HEADS = 128
KV_HEADS = 8
HEAD_DIM = 128
TENANTS = 4
ROPE_BASE = 500000.0
ADAPTER_ALPHA = 8.0


def product(left, right):
    return jnp.dot(left, right, preferred_element_type=jnp.float32)


def rotate_pairs(values, position, first_col):
    pair_count = values.shape[1] // 2
    pair_col = first_col + 2 * jnp.arange(pair_count, dtype=jnp.int32)
    within = pair_col % HEAD_DIM // 2
    frequency = jnp.exp(-(2.0 * within.astype(jnp.float32) / HEAD_DIM) * math.log(ROPE_BASE))
    angles = position.astype(jnp.float32)[:, None] * frequency[None, :]
    pair_view = values.reshape(values.shape[0], pair_count, 2)
    even_part = pair_view[:, :, 0]
    odd_part = pair_view[:, :, 1]
    cosine = jnp.cos(angles)
    sine_angle = jnp.sin(angles)
    turned = jnp.stack(
        [even_part * cosine - odd_part * sine_angle, even_part * sine_angle + odd_part * cosine],
        axis=2,
    )
    return turned.reshape(values.shape)


def tenant_table(token_ids, adapter_rank, token_lengths, adapter_slot):
    segment_ends = jnp.cumsum(token_lengths)
    begins = segment_ends - token_lengths
    owned_rows = (token_ids[:, None] >= begins[None, :]) & (
        token_ids[:, None] < segment_ends[None, :]
    )
    zero_int = jnp.zeros((), jnp.int32)
    own_rank = jnp.sum(jnp.where(owned_rows, adapter_rank[None, :], zero_int), axis=1)
    own_slot = jnp.sum(jnp.where(owned_rows, adapter_slot[None, :], zero_int), axis=1)
    own_first = jnp.sum(jnp.where(owned_rows, begins[None, :], zero_int), axis=1)
    slot_hot = own_slot[:, None] == jnp.arange(TENANTS, dtype=jnp.int32)[None, :]
    return (own_rank, own_first, slot_hot)


def select_slot(down_values, slot_hot):
    shaped = down_values.reshape(down_values.shape[0], -1, TENANTS)
    return jnp.sum(jnp.where(slot_hot[:, None, :], shaped, 0.0), axis=2)


def scale_ranks(picked, own_rank, first_rank):
    rank_index = first_rank + jnp.arange(picked.shape[1], dtype=jnp.int32)
    keep_mask = rank_index[None, :] < own_rank[:, None]
    factor = ADAPTER_ALPHA / jnp.sqrt(own_rank.astype(jnp.float32))
    return jnp.where(keep_mask, picked * factor[:, None], 0.0).astype(jnp.bfloat16)


def widen_slots(low_values, slot_hot):
    wide_rows = jnp.where(
        slot_hot[:, None, :], low_values[:, :, None], jnp.zeros((), low_values.dtype)
    )
    return wide_rows.reshape(low_values.shape[0], -1)


def shards(
    tokens,
    weight_query,
    weight_keyval,
    down_query,
    down_keyval,
    up_query,
    up_keyval,
    adapter_rank,
    token_lengths,
    adapter_slot,
):
    ring = lax.axis_size("tensor")
    split = lax.axis_size(("seq", "load"))
    tensor_index = lax.axis_index("tensor")
    block_index = lax.axis_index(("seq", "load"))
    query_cols = weight_query.shape[1]
    keyval_cols = weight_keyval.shape[1]
    rank_share = down_query.shape[1] // TENANTS
    chunk = tokens.shape[0]
    piece = chunk // split
    local_rows = ring * piece
    up_query_all = lax.all_gather(up_query, "load", axis=0, tiled=True)
    up_keyval_all = lax.all_gather(up_keyval, "load", axis=0, tiled=True)
    shift = [(i, (i + 1) % ring) for i in range(ring)]
    held = tokens
    reduced = []
    for step in range(ring):
        following = lax.ppermute(held, "tensor", shift) if step < ring - 1 else None
        owner = (tensor_index - step) % ring
        block_ids = owner * chunk + jnp.arange(chunk, dtype=jnp.int32)
        _, _, block_hot = tenant_table(block_ids, adapter_rank, token_lengths, adapter_slot)
        partial = jnp.concatenate(
            [
                product(held, weight_query),
                product(held, weight_keyval),
                select_slot(product(held, down_query), block_hot),
                select_slot(product(held, down_keyval), block_hot),
            ],
            axis=1,
        )
        reduced.append(lax.psum_scatter(partial, ("seq", "load"), scatter_dimension=0, tiled=True))
        held = following
    steps_of_owner = (tensor_index - jnp.arange(ring, dtype=jnp.int32)) % ring
    summed = jnp.take(jnp.stack(reduced), steps_of_owner, axis=0).reshape(local_rows, -1)
    owners = jnp.arange(ring, dtype=jnp.int32)
    piece_ids = jnp.arange(piece, dtype=jnp.int32)
    token_ids = (owners[:, None] * chunk + block_index * piece + piece_ids[None, :]).reshape(-1)
    own_rank, own_first, slot_hot = tenant_table(
        token_ids, adapter_rank, token_lengths, adapter_slot
    )
    position = token_ids - own_first
    low_start = query_cols + keyval_cols
    first_rank = tensor_index * rank_share
    low_query = scale_ranks(summed[:, low_start : low_start + rank_share], own_rank, first_rank)
    low_keyval = scale_ranks(summed[:, low_start + rank_share :], own_rank, first_rank)
    low_both = lax.all_gather(jnp.concatenate([low_query, low_keyval], axis=1), "tensor", axis=1)
    full_query = low_both[:, :, :rank_share].reshape(local_rows, -1)
    full_keyval = low_both[:, :, rank_share:].reshape(local_rows, -1)
    wide_query = widen_slots(full_query, slot_hot)
    wide_keyval = widen_slots(full_keyval, slot_hot)
    delta_query = product(wide_query, up_query_all)
    delta_keyval = product(wide_keyval, up_keyval_all)
    query_rows = rotate_pairs(
        summed[:, :query_cols] + delta_query, position, tensor_index * query_cols
    ).astype(jnp.bfloat16)
    keyval = summed[:, query_cols:low_start] + delta_keyval
    kv_first_col = tensor_index * keyval_cols
    is_key = kv_first_col + jnp.arange(keyval_cols, dtype=jnp.int32) < KV_HEADS * HEAD_DIM
    kv_local = jnp.where(
        is_key[None, :], rotate_pairs(keyval, position, kv_first_col), keyval
    ).astype(jnp.bfloat16)
    kv_all = lax.all_gather(kv_local, "tensor", axis=1, tiled=True)
    heads_here = query_cols // HEAD_DIM
    group_size = HEADS // KV_HEADS
    kv_here = max(heads_here // group_size, 1)
    per_kv = heads_here // kv_here
    kv_first = tensor_index * heads_here // group_size
    key_cols = KV_HEADS * HEAD_DIM
    key_heads = lax.dynamic_slice_in_dim(
        kv_all, kv_first * HEAD_DIM, kv_here * HEAD_DIM, 1
    ).reshape(local_rows, kv_here, HEAD_DIM)
    value_heads = lax.dynamic_slice_in_dim(
        kv_all, key_cols + kv_first * HEAD_DIM, kv_here * HEAD_DIM, 1
    ).reshape(local_rows, kv_here, HEAD_DIM)
    both_heads = lax.all_gather(
        jnp.concatenate([key_heads, value_heads], axis=1), ("seq", "load"), axis=0, tiled=True
    )
    piece_keys = both_heads[:, :kv_here]
    piece_values = both_heads[:, kv_here:]
    key_ids = (
        owners[None, :, None] * chunk
        + jnp.arange(split, dtype=jnp.int32)[:, None, None] * piece
        + piece_ids[None, None, :]
    ).reshape(-1)
    grouped = query_rows.reshape(local_rows, kv_here, per_kv, HEAD_DIM)
    visible = (key_ids[None, :] >= own_first[:, None]) & (key_ids[None, :] <= token_ids[:, None])
    scores = jnp.einsum(
        "qghd,kgd->ghqk", grouped, piece_keys, preferred_element_type=jnp.float32
    ) / math.sqrt(HEAD_DIM)
    scores = jnp.where(visible, scores, -1e30)
    row_top = jnp.max(scores, axis=3)
    exp_scores = jnp.where(visible, jnp.exp(scores - row_top[..., None]), 0.0)
    row_total = jnp.sum(exp_scores, axis=3)
    accumulated = jnp.einsum(
        "ghqk,kgd->ghqd",
        exp_scores.astype(jnp.bfloat16),
        piece_values,
        preferred_element_type=jnp.float32,
    )
    context = (accumulated / row_total[..., None]).astype(jnp.bfloat16)
    context = jnp.transpose(context, (2, 0, 1, 3)).reshape(local_rows, query_cols)
    outgoing = jnp.concatenate([context, kv_local], axis=1)
    by_owner = outgoing.reshape(split, ring // split, piece, -1)
    arrived = lax.all_to_all(by_owner, ("seq", "load"), 0, 0)
    placed = jnp.transpose(arrived, (1, 0, 2, 3)).reshape(local_rows, -1)
    return (placed[:, :query_cols], placed[:, query_cols:])


def solution(mesh):
    placed = (
        P(("groups", "tensor"), ("seq", "load")),
        P(("seq", "load"), "tensor"),
        P(("seq", "load"), "tensor"),
        P(("seq", "load"), ("groups", "tensor")),
        P(("seq", "load"), ("groups", "tensor")),
        P(("groups", "load"), "tensor"),
        P(("groups", "load"), "tensor"),
        P("groups"),
        P("groups"),
        P("groups"),
    )
    return jax.shard_map(
        shards,
        mesh=mesh,
        in_specs=placed,
        out_specs=(P(("groups", "seq", "load"), "tensor"), P(("groups", "seq", "load"), "tensor")),
        check_vma=False,
    )
```

profile of v0, /device:TPU:0, one launch (start us, length us, event | category | flops | bytes accessed | tf_op | source)
XLA Modules:
  0.0 315.2 jit_solution(80680660956528715)
XLA Ops:
  8.1 0.9 reduce-window.8
  9.0 0.7 bitcast_subtract_fusion
  9.9 16.9 %fusion.47 = f32[128,4096]{1,0:T(8,128)} fusion(bf16[128,4096]{1,0:T(8,128)(2,1)} %param.10, bf16[4096,4096]{1,0:T(8,128)(2,1)} %param.11), kind=kOutput, calls=%fused_computation.135 | convolution fusion | flops 4294967296 | bytes 36700160 | tf_op jit(solution)/shard_map/dot_general | solution.py:16
  26.7 0.8 fusion.48
  27.6 0.5 fusion.50
  28.1 0.5 fusion.49
  29.1 3.6 %concatenate.26 = f32[128,4672]{1,0:T(8,128)} concatenate(f32[128,4096]{1,0:T(8,128)} %fusion.47, f32[128,512]{1,0:T(8,128)S(1)} %fusion.48, f32[128,32]{1,0:T(8,128)S(1)} %copy.64, f32[128,32]{1,0:T(8,128)S(1)} %copy.65), dimensions={1} | concatenate | bytes 4784128 | tf_op jit(solution)/shard_map/concatenate | solution.py:102
  32.7 3.1 collective-permute-start
  35.8 25.2 %collective-permute-done = bf16[128,4096]{1,0:T(8,128)(2,1)S(1)} collective-permute-done((bf16[128,4096]{1,0:T(8,128)(2,1)S(1)}, bf16[128,4096]{1,0:T(8,128)(2,1)S(1)}, u32[]{:S(2)}, u32[]{:S(2)}) %collective-permute-start) | collective-permute-done | bytes 1048608 | tf_op jit(solution)/shard_map/ppermute | solution.py:98
  61.5 1.7 fusion.53
  63.6 2.9 fusion.52
  66.5 14.3 %fusion.51 = f32[128,4096]{1,0:T(8,128)} fusion(bf16[128,4096]{1,0:T(8,128)(2,1)S(1)} %collective-permute-done, bf16[4096,4096]{1,0:T(8,128)(2,1)} %param.11), kind=kOutput, calls=%fused_computation.139 | convolution fusion | flops 4294967296 | bytes 36700160 | tf_op jit(solution)/shard_map/dot_general | solution.py:16
  80.8 3.6 %concatenate.27 = f32[128,4672]{1,0:T(8,128)} concatenate(f32[128,4096]{1,0:T(8,128)} %fusion.51, f32[128,512]{1,0:T(8,128)S(1)} %fusion.52, f32[128,32]{1,0:T(8,128)S(1)} %copy.66, f32[128,32]{1,0:T(8,128)S(1)} %copy.67), dimensions={1} | concatenate | bytes 4784128 | tf_op jit(solution)/shard_map/concatenate | solution.py:102
  84.7 26.1 %collective-permute-done.1 = bf16[128,4096]{1,0:T(8,128)(2,1)S(1)} collective-permute-done((bf16[128,4096]{1,0:T(8,128)(2,1)S(1)}, bf16[128,4096]{1,0:T(8,128)(2,1)S(1)}, u32[]{:S(2)}, u32[]{:S(2)}) %collective-permute-start.1) | collective-permute-done | bytes 1048608 | tf_op jit(solution)/shard_map/ppermute | solution.py:98
  111.4 1.7 fusion.57
  113.4 3.0 fusion.56
  116.4 14.3 %fusion.55 = f32[128,4096]{1,0:T(8,128)} fusion(bf16[128,4096]{1,0:T(8,128)(2,1)S(1)} %collective-permute-done.1, bf16[4096,4096]{1,0:T(8,128)(2,1)} %param.11), kind=kOutput, calls=%fused_computation.143 | convolution fusion | flops 4294967296 | bytes 36700160 | tf_op jit(solution)/shard_map/dot_general | solution.py:16
  130.7 3.6 %concatenate.28 = f32[128,4672]{1,0:T(8,128)} concatenate(f32[128,4096]{1,0:T(8,128)} %fusion.55, f32[128,512]{1,0:T(8,128)S(1)} %fusion.56, f32[128,32]{1,0:T(8,128)S(1)} %copy.68, f32[128,32]{1,0:T(8,128)S(1)} %copy.69), dimensions={1} | concatenate | bytes 4784128 | tf_op jit(solution)/shard_map/concatenate | solution.py:102
  134.5 25.2 %collective-permute-done.2 = bf16[128,4096]{1,0:T(8,128)(2,1)S(1)} collective-permute-done((bf16[128,4096]{1,0:T(8,128)(2,1)S(1)}, bf16[128,4096]{1,0:T(8,128)(2,1)S(1)}, u32[]{:S(2)}, u32[]{:S(2)}) %collective-permute-start.2) | collective-permute-done | bytes 1048608 | tf_op jit(solution)/shard_map/ppermute | solution.py:98
  160.2 1.7 fusion.61
  162.2 2.9 fusion.60
  165.2 14.3 %fusion.59 = f32[128,4096]{1,0:T(8,128)} fusion(bf16[128,4096]{1,0:T(8,128)(2,1)S(1)} %collective-permute-done.2, bf16[4096,4096]{1,0:T(8,128)(2,1)} %param.11), kind=kOutput, calls=%fused_computation.147 | convolution fusion | flops 4294967296 | bytes 36700160 | tf_op jit(solution)/shard_map/dot_general | solution.py:16
  179.5 3.6 %concatenate.29 = f32[128,4672]{1,0:T(8,128)} concatenate(f32[128,4096]{1,0:T(8,128)} %fusion.59, f32[128,512]{1,0:T(8,128)S(1)} %fusion.60, f32[128,32]{1,0:T(8,128)S(1)} %copy.70, f32[128,32]{1,0:T(8,128)S(1)} %copy.71), dimensions={1} | concatenate | bytes 4784128 | tf_op jit(solution)/shard_map/concatenate | solution.py:102
  183.7 0.6 multiply_exponential_fusion
  184.3 0.5 add_compare_fusion
  185.0 2.5 all_gather.20
  188.6 25.8 %reduce-scatter.11.cloned.1.call-done = f32[32,4672]{1,0:T(8,128)} async-done(((f32[128,4672]{1,0:T(8,128)}), f32[32,4672]{1,0:T(8,128)}) %reduce-scatter.11.cloned.1.call-update) | async-done | bytes 598032 | tf_op jit(solution)/shard_map/reduce_scatter | solution.py:111
  214.4 1.8 pad_maximum_fusion
  216.2 2.2 gather_fusion
  218.3 1.9 bitcast_select_fusion.4
  220.6 13.5 %all-gather = bf16[128,256]{0,1:T(8,128)(2,1)S(1)} all-gather(bf16[128,64]{0,1:T(8,128)(2,1)S(1)} %copy.72), channel_id=2, replica_groups=mesh['groups'=2,'tensor'=4,'seq'=2,'load'=2] {'tensor'}, dimensions={1}, use_global_device_ids=true | all-gather | bytes 81920 | tf_op jit(solution)/shard_map/all_gather | solution.py:126
  235.0 1.2 fusion.25
  236.4 0.8 copy.77
  237.2 4.3 %convolution_add_fusion = f32[128,4096]{1,0:T(8,128)} fusion(bf16[128,512]{0,1:T(8,128)(2,1)S(1)} %bitcast.120, bf16[512,4096]{1,0:T(8,128)(2,1)} %all-gather.3.cloned.1.call-done, f32[128,4672]{1,0:T(8,128)S(1)} %bitcast_select_fusion.4), kind=kOutput, calls=%fused_computation.5 | convolution fusion | flops 537395200 | bytes 8519680 | tf_op jit(solution)/shard_map/dot_general | solution.py:16
  241.5 1.9 copy.82
  243.4 2.6 fusion.43
  246.0 2.4 copy.97
  248.5 0.7 copy.96
  249.1 4.2 %fusion.15 = (bf16[128,2048,1]{1,0,2:T(8,128)(2,1)S(1)}, bf16[128,2048,1]{1,0,2:T(8,128)(2,1)S(1)}) fusion(f32[128,2048,1]{1,0,2:T(8,128)S(1)} %copy.97, f32[128,2048,1]{1,0,2:T(8,128)S(1)} %copy.96, f32[2048]{0:T(1024)S(1)} %fusion.35, f32[128]{0:T(128)S(1)} %copy-done.10), kind=kLoop, calls=%fused_computation.24 | loop fusion | flops 2359296 | bytes 3154432 | tf_op jit(solution)/shard_map/convert
  253.5 0.8 copy.85
  254.4 16.0 %all_gather.21 = bf16[128,2048]{1,0:T(8,128)(2,1)S(1)} all-gather(bf16[128,512]{1,0:T(8,128)(2,1)S(1)} %select_convert_fusion), channel_id=1, replica_groups=mesh['groups'=2,'tensor'=4,'seq'=2,'load'=2] {'tensor'}, dimensions={1}, use_global_device_ids=true | all-gather | bytes 655360 | tf_op jit(solution)/shard_map/all_gather | solution.py:142
  270.9 6.5 %all_gather.22 = bf16[512,4,128]{2,0,1:T(8,128)(2,1)S(1)} all-gather(bf16[128,4,128]{2,0,1:T(8,128)(2,1)S(1)} %pad_maximum_fusion.3), channel_id=1, replica_groups=mesh['groups'=2,'tensor'=4,'seq'=2,'load'=2] {'seq','load'}, dimensions={0}, use_global_device_ids=true | all-gather | bytes 655360 | tf_op jit(solution)/shard_map/all_gather | solution.py:155
  277.4 5.1 %fusion.46 = (f32[2,16,128]{2,1,0:T(8,128)S(1)}, bf16[2,16,128,512]{2,3,1,0:T(8,128)(2,1)}) fusion(pred[128,512]{0,1:T(8,128)(4,1)S(1)} %compare_and_fusion, bf16[128,2,16,128]{0,3,2,1:T(8,128)(2,1)S(1)} %bitcast.114, bf16[512,4,128]{2,0,1:T(8,128)(2,1)S(1)} %all_gather.22), kind=kOutput, calls=%fused_computation.134 | convolution fusion | flops 549454336 | bytes 5652480 | tf_op jit(solution)/shard_map/sub | solution.py:172
  282.5 4.1 %fusion.7 = bf16[128,2,16,128]{3,0,2,1:T(8,128)(2,1)S(1)} fusion(bf16[2,16,128,512]{2,3,1,0:T(8,128)(2,1)} %get-tuple-element.34, f32[128,2,16]{0,2,1:T(8,128)S(1)} %bitcast.138, bf16[512,4,128]{2,0,1:T(8,128)(2,1)S(1)} %all_gather.22), kind=kOutput, calls=%fused_computation.14 | convolution fusion | flops 537919488 | bytes 5521408 | tf_op jit(solution)/shard_map/ghqk,kgd->ghqd/dot_general | solution.py:174
  286.6 0.7 copy.88
  287.9 18.4 %all_to_all.5 = bf16[4,1,32,4608]{3,2,1,0:T(8,128)(2,1)S(1)} all-to-all(bf16[4,1,32,4608]{3,2,1,0:T(8,128)(2,1)S(1)} %maximum_bitcast_fusion), channel_id=1, replica_groups=mesh['groups'=2,'tensor'=4,'seq'=2,'load'=2] {'seq','load'}, dimensions={0} | all-to-all | bytes 2359296 | tf_op jit(solution)/shard_map/all_to_all | solution.py:184
  306.3 1.1 slice.70
  307.4 0.7 slice.71
  (107 shorter events, 7.9 us)
Async XLA Ops:
  8.0 19.5 %copy-start = (bf16[4096,128]{1,0:T(8,128)(2,1)S(1)}, bf16[4096,128]{1,0:T(8,128)(2,1)}, u32[]{:S(2)}) copy-start(bf16[4096,128]{1,0:T(8,128)(2,1)} %param.14) | copy-start | bytes 3145732
  8.0 180.5 %reduce-scatter.5.cloned.1.call-start = ((), (), s32[]{:S(2)}) async-start(), calls=%async_computation.5 | async-start | bytes 3031040 | tf_op jit(solution)/shard_map/reduce_scatter | solution.py:111
  9.9 16.9 %copy-start.2 = (bf16[4096,512]{1,0:T(8,128)(2,1)S(1)}, bf16[4096,512]{1,0:T(8,128)(2,1)}, u32[]{:S(2)}) copy-start(bf16[4096,512]{1,0:T(8,128)(2,1)} %param.12) | copy-start | bytes 12582916
  9.9 16.9 %copy-start.3 = (bf16[128,4096]{1,0:T(8,128)(2,1)S(1)}, bf16[128,4096]{1,0:T(8,128)(2,1)}, u32[]{:S(2)}) copy-start(bf16[128,4096]{1,0:T(8,128)(2,1)} %param.10) | copy-start | bytes 3145732
  26.7 1.4 copy-start.4
  27.5 1.1 copy-start.12
  27.6 1.1 copy-start.13
  32.7 155.9 %reduce-scatter.7.cloned.1.call-start = ((), (), s32[]{:S(2)}) async-start(), calls=%async_computation.6 | async-start | bytes 3031040 | tf_op jit(solution)/shard_map/reduce_scatter | solution.py:111
  32.7 28.3 %collective-permute-start = (bf16[128,4096]{1,0:T(8,128)(2,1)S(1)}, bf16[128,4096]{1,0:T(8,128)(2,1)S(1)}, u32[]{:S(2)}, u32[]{:S(2)}) collective-permute-start(bf16[128,4096]{1,0:T(8,128)(2,1)S(1)} %copy-done.3), channel_id=1, source_target_pairs={{0,4},{4,8},{8,12},{12,0},{1,5},{5,9},{9,13},{13,1},{2,6},{6,10},{... | collective-permute-start | bytes 3145736 | tf_op jit(solution)/shard_map/ppermute | solution.py:98
  84.4 104.1 %reduce-scatter.9.cloned.1.call-start = ((), (), s32[]{:S(2)}) async-start(), calls=%async_computation.7 | async-start | bytes 3031040 | tf_op jit(solution)/shard_map/reduce_scatter | solution.py:111
  84.5 26.4 %collective-permute-start.1 = (bf16[128,4096]{1,0:T(8,128)(2,1)S(1)}, bf16[128,4096]{1,0:T(8,128)(2,1)S(1)}, u32[]{:S(2)}, u32[]{:S(2)}) collective-permute-start(bf16[128,4096]{1,0:T(8,128)(2,1)S(1)} %collective-permute-done), channel_id=1, source_target_pairs={{0,4},{4,8},{8,12},{12,0},{1,5},{5,9},{9,13},{13,1},{2,6},{6,10},{... | collective-permute-start | bytes 3145736 | tf_op jit(solution)/shard_map/ppermute | solution.py:98
  134.3 80.0 %reduce-scatter.11.cloned.1.call-start = ((), (), s32[]{:S(2)}) async-start(), calls=%async_computation.8 | async-start | bytes 3031040 | tf_op jit(solution)/shard_map/reduce_scatter | solution.py:111
  134.4 25.2 %collective-permute-start.2 = (bf16[128,4096]{1,0:T(8,128)(2,1)S(1)}, bf16[128,4096]{1,0:T(8,128)(2,1)S(1)}, u32[]{:S(2)}, u32[]{:S(2)}) collective-permute-start(bf16[128,4096]{1,0:T(8,128)(2,1)S(1)} %collective-permute-done.1), channel_id=1, source_target_pairs={{0,4},{4,8},{8,12},{12,0},{1,5},{5,9},{9,13},{13,1},{2,6},{6,10},{... | collective-permute-start | bytes 3145736 | tf_op jit(solution)/shard_map/ppermute | solution.py:98
  183.1 1.9 copy-start.9
  183.1 54.1 %all-gather.3.cloned.1.call-start = ((), (), s32[]{:S(2)}) async-start(), calls=%async_computation.9 | async-start | bytes 6291456 | tf_op jit(solution)/shard_map/all_gather | solution.py:92
  220.4 14.6 %copy-start.10 = (f32[128]{0:T(128)S(1)}, f32[128]{0:T(128)}, u32[]{:S(2)}) copy-start(f32[128]{0:T(128)} %subtract_convert_fusion) | copy-start | bytes 1540
  234.5 7.0 %copy-start.6 = (f32[128,512]{1,0:T(8,128)}, f32[128,512]{1,0:T(8,128)S(1)}, u32[]{:S(2)}) copy-start(f32[128,512]{1,0:T(8,128)S(1)} %convolution_add_fusion.1) | copy-start | bytes 786436
  246.0 2.4 copy-start.5
  253.4 1.0 copy-start.7
  253.4 1.0 copy-start.8
  253.4 1.0 copy-start.11
  287.8 20.3 %copy-start.1 = (bf16[4096,128]{1,0:T(8,128)(2,1)S(1)}, bf16[4096,128]{1,0:T(8,128)(2,1)}, u32[]{:S(2)}) copy-start(bf16[4096,128]{1,0:T(8,128)(2,1)} %param.14) | copy-start | bytes 3145732
Sparse Core Ops, SparseCore 0:
  32.8 36.1 reduce-scatter.4
  84.6 32.8 reduce-scatter.6
  134.5 31.3 reduce-scatter.8
  183.2 31.1 reduce-scatter.10
Sparse Core Ops, SparseCore 1:
  185.1 11.2 all-gather.2
where the time goes:
time: 316 us; the launch traced here: 315 us
  waiting for transfers between devices  103 us (33%)
  matrix products  91 us (29%)
  blocking collectives  56.9 us (18%)
  local copies, waits for them, and re-layouts  31 us (10%)
  between operations  15.9 us (5%)
  other arithmetic  13.9 us (4%)
  starting transfers between devices  3.57 us (1%)
    dot_general x18, matrix products, product(): return jnp.dot(left, right, preferred_element_type=jnp.float32)  81.8 us
    ppermute x3, waiting for transfers between devices, shards(): following = lax.ppermute(held, 'tensor', shift) if step < ring - 1 else None  76.5 us
    reduce_scatter x4, waiting for transfers between devices, shards(): lax.psum_scatter(partial, ('seq', 'load'), scatter_dimension=0, tiled=True)  25.9 us
    all_to_all x1, blocking collectives, shards(): arrived = lax.all_to_all(by_owner, ('seq', 'load'), 0, 0)  18.4 us
    all_gather x1, blocking collectives, shards(): kv_all = lax.all_gather(kv_local, 'tensor', axis=1, tiled=True)  16 us
    concatenate x4, local copies, waits for them, and re-layouts, shards(): jnp.concatenate([product(held, weight_query), product(held, weight_keyval...  14.3 us
    all_gather x1, blocking collectives, shards(): lax.all_gather(jnp.concatenate([low_query, low_keyval], axis=1), 'tensor'...  13.5 us
    all_gather x1, blocking collectives, shards(): lax.all_gather(jnp.concatenate([key_heads, value_heads], axis=1), ('seq',...  6.51 us
  transfers between devices with their start and end apart: 8, of which 4 were waited for; matrix products, arithmetic and copies ran while one was open for 26% of the time, Pallas kernels for 0%

commit v1 on v0

--- a/solution.py
+++ b/solution.py
@@ -139,7 +139,15 @@
     kv_local = jnp.where(
         is_key[None, :], rotate_pairs(keyval, position, kv_first_col), keyval
     ).astype(jnp.bfloat16)
-    kv_all = lax.all_gather(kv_local, "tensor", axis=1, tiled=True)
+    ways, here = (lax.axis_size("tensor"), lax.axis_index("tensor"))
+    grown, reach = (kv_local, 1)
+    while reach < ways:
+        theirs = lax.ppermute(grown, "tensor", [(d, d ^ reach) for d in range(ways)])
+        mine_first = jnp.concatenate([grown, theirs], axis=1)
+        theirs_first = jnp.concatenate([theirs, grown], axis=1)
+        grown = jnp.where(here & reach == 0, mine_first, theirs_first)
+        reach = 2 * reach
+    kv_all = grown
     heads_here = query_cols // HEAD_DIM
     group_size = HEADS // KV_HEADS
     kv_here = max(heads_here // group_size, 1)

time: 316 us -> 307 us (0.972)
  blocking collectives: 56.9 us -> 41 us
  waiting for transfers between devices: 103 us -> 107 us
  starting transfers between devices: 3.57 us -> 7.54 us
    all_gather x1 -> x0, blocking collectives: 16 us -> none  [shards(): kv_all = lax.all_gather(kv_local, 'tensor', axis=1, tiled=True)]
    ppermute x0 -> x2, starting transfers between devices: none -> 3.97 us  [shards(): lax.ppermute(grown, 'tensor', [(d, d ^ reach) for d in range(ways)])]
    ppermute x0 -> x2, waiting for transfers between devices: none -> 3.84 us  [shards(): lax.ppermute(grown, 'tensor', [(d, d ^ reach) for d in range(ways)])]
  transfers between devices with their start and end apart: 8 -> 10, of which waited for: 4 -> 5; matrix products, arithmetic and copies ran while one was open for 26% -> 30% of each run, Pallas kernels for 0% -> 0%
where the time goes in v1:
time: 307 us
  waiting for transfers between devices  107 us (35%)
  matrix products  91 us (30%)
  blocking collectives  41 us (13%)
  local copies, waits for them, and re-layouts  30.3 us (10%)
  between operations  15.9 us (5%)
  other arithmetic  14 us (5%)
  starting transfers between devices  7.54 us (2%)
    dot_general x18, matrix products, product(): return jnp.dot(left, right, preferred_element_type=jnp.float32)  81.8 us
    ppermute x3, waiting for transfers between devices, shards(): following = lax.ppermute(held, 'tensor', shift) if step < ring - 1 else None  76.5 us
    reduce_scatter x4, waiting for transfers between devices, shards(): lax.psum_scatter(partial, ('seq', 'load'), scatter_dimension=0, tiled=True)  25.9 us
    all_to_all x1, blocking collectives, shards(): arrived = lax.all_to_all(by_owner, ('seq', 'load'), 0, 0)  18.4 us
    concatenate x4, local copies, waits for them, and re-layouts, shards(): jnp.concatenate([product(held, weight_query), product(held, weight_keyval...  14.3 us
    all_gather x1, blocking collectives, shards(): lax.all_gather(jnp.concatenate([low_query, low_keyval], axis=1), 'tensor'...  13.5 us
    all_gather x1, blocking collectives, shards(): lax.all_gather(jnp.concatenate([key_heads, value_heads], axis=1), ('seq',...  6.51 us
  transfers between devices with their start and end apart: 10, of which 5 were waited for; matrix products, arithmetic and copies ran while one was open for 30% of the time, Pallas kernels for 0%

profile of v1, /device:TPU:0, one launch (start us, length us, event | category | flops | bytes accessed | tf_op | source)
XLA Modules:
  0.0 306.6 jit_solution(17904640142912354843)
XLA Ops:
  8.1 0.9 reduce-window.8
  9.0 0.7 bitcast_subtract_fusion
  9.9 16.9 %fusion.47 = f32[128,4096]{1,0:T(8,128)} fusion(bf16[128,4096]{1,0:T(8,128)(2,1)} %param.10, bf16[4096,4096]{1,0:T(8,128)(2,1)} %param.11), kind=kOutput, calls=%fused_computation.137 | convolution fusion | flops 4294967296 | bytes 36700160 | tf_op jit(solution)/shard_map/dot_general | solution.py:16
  26.7 0.8 fusion.48
  28.1 0.5 fusion.49
  29.1 3.6 %concatenate.38 = f32[128,4672]{1,0:T(8,128)} concatenate(f32[128,4096]{1,0:T(8,128)} %fusion.47, f32[128,512]{1,0:T(8,128)S(1)} %fusion.48, f32[128,32]{1,0:T(8,128)S(1)} %copy.64, f32[128,32]{1,0:T(8,128)S(1)} %copy.65), dimensions={1} | concatenate | bytes 4784128 | tf_op jit(solution)/shard_map/concatenate | solution.py:102
  32.7 3.1 %collective-permute-start = (bf16[128,4096]{1,0:T(8,128)(2,1)S(1)}, bf16[128,4096]{1,0:T(8,128)(2,1)S(1)}, u32[]{:S(2)}, u32[]{:S(2)}) collective-permute-start(bf16[128,4096]{1,0:T(8,128)(2,1)S(1)} %copy-done.3), channel_id=1, source_target_pairs={{0,4},{4,8},{8,12},{12,0},{1,5},{5,9},{9,13},{13,1},{2,6},{6,10},{... | collective-permute-start | bytes 3145736 | tf_op jit(solution)/shard_map/ppermute | solution.py:98
  35.8 25.2 %collective-permute-done = bf16[128,4096]{1,0:T(8,128)(2,1)S(1)} collective-permute-done((bf16[128,4096]{1,0:T(8,128)(2,1)S(1)}, bf16[128,4096]{1,0:T(8,128)(2,1)S(1)}, u32[]{:S(2)}, u32[]{:S(2)}) %collective-permute-start) | collective-permute-done | bytes 1048608 | tf_op jit(solution)/shard_map/ppermute | solution.py:98
  61.5 1.7 fusion.53
  63.6 2.9 fusion.52
  66.5 14.3 %fusion.51 = f32[128,4096]{1,0:T(8,128)} fusion(bf16[128,4096]{1,0:T(8,128)(2,1)S(1)} %collective-permute-done, bf16[4096,4096]{1,0:T(8,128)(2,1)} %param.11), kind=kOutput, calls=%fused_computation.141 | convolution fusion | flops 4294967296 | bytes 36700160 | tf_op jit(solution)/shard_map/dot_general | solution.py:16
  80.8 3.6 %concatenate.39 = f32[128,4672]{1,0:T(8,128)} concatenate(f32[128,4096]{1,0:T(8,128)} %fusion.51, f32[128,512]{1,0:T(8,128)S(1)} %fusion.52, f32[128,32]{1,0:T(8,128)S(1)} %copy.66, f32[128,32]{1,0:T(8,128)S(1)} %copy.67), dimensions={1} | concatenate | bytes 4784128 | tf_op jit(solution)/shard_map/concatenate | solution.py:102
  84.7 26.1 %collective-permute-done.1 = bf16[128,4096]{1,0:T(8,128)(2,1)S(1)} collective-permute-done((bf16[128,4096]{1,0:T(8,128)(2,1)S(1)}, bf16[128,4096]{1,0:T(8,128)(2,1)S(1)}, u32[]{:S(2)}, u32[]{:S(2)}) %collective-permute-start.1) | collective-permute-done | bytes 1048608 | tf_op jit(solution)/shard_map/ppermute | solution.py:98
  111.4 1.7 fusion.57
  113.4 3.0 fusion.56
  116.4 14.3 %fusion.55 = f32[128,4096]{1,0:T(8,128)} fusion(bf16[128,4096]{1,0:T(8,128)(2,1)S(1)} %collective-permute-done.1, bf16[4096,4096]{1,0:T(8,128)(2,1)} %param.11), kind=kOutput, calls=%fused_computation.145 | convolution fusion | flops 4294967296 | bytes 36700160 | tf_op jit(solution)/shard_map/dot_general | solution.py:16
  130.7 3.6 %concatenate.40 = f32[128,4672]{1,0:T(8,128)} concatenate(f32[128,4096]{1,0:T(8,128)} %fusion.55, f32[128,512]{1,0:T(8,128)S(1)} %fusion.56, f32[128,32]{1,0:T(8,128)S(1)} %copy.68, f32[128,32]{1,0:T(8,128)S(1)} %copy.69), dimensions={1} | concatenate | bytes 4784128 | tf_op jit(solution)/shard_map/concatenate | solution.py:102
  134.5 25.2 %collective-permute-done.2 = bf16[128,4096]{1,0:T(8,128)(2,1)S(1)} collective-permute-done((bf16[128,4096]{1,0:T(8,128)(2,1)S(1)}, bf16[128,4096]{1,0:T(8,128)(2,1)S(1)}, u32[]{:S(2)}, u32[]{:S(2)}) %collective-permute-start.2) | collective-permute-done | bytes 1048608 | tf_op jit(solution)/shard_map/ppermute | solution.py:98
  160.2 1.7 fusion.61
  162.2 2.9 fusion.60
  165.2 14.3 %fusion.59 = f32[128,4096]{1,0:T(8,128)} fusion(bf16[128,4096]{1,0:T(8,128)(2,1)S(1)} %collective-permute-done.2, bf16[4096,4096]{1,0:T(8,128)(2,1)} %param.11), kind=kOutput, calls=%fused_computation.149 | convolution fusion | flops 4294967296 | bytes 36700160 | tf_op jit(solution)/shard_map/dot_general | solution.py:16
  179.5 3.6 %concatenate.41 = f32[128,4672]{1,0:T(8,128)} concatenate(f32[128,4096]{1,0:T(8,128)} %fusion.59, f32[128,512]{1,0:T(8,128)S(1)} %fusion.60, f32[128,32]{1,0:T(8,128)S(1)} %copy.70, f32[128,32]{1,0:T(8,128)S(1)} %copy.71), dimensions={1} | concatenate | bytes 4784128 | tf_op jit(solution)/shard_map/concatenate | solution.py:102
  183.7 0.6 multiply_exponential_fusion
  184.3 0.5 add_compare_fusion
  185.0 2.5 all_gather.17
  188.6 25.8 %reduce-scatter.11.cloned.1.call-done = f32[32,4672]{1,0:T(8,128)} async-done(((f32[128,4672]{1,0:T(8,128)}), f32[32,4672]{1,0:T(8,128)}) %reduce-scatter.11.cloned.1.call-update) | async-done | bytes 598032 | tf_op jit(solution)/shard_map/reduce_scatter | solution.py:111
  214.4 1.8 pad_maximum_fusion
  216.2 2.2 gather_fusion
  218.3 1.9 bitcast_select_fusion.4
  220.6 13.5 %all-gather = bf16[128,256]{0,1:T(8,128)(2,1)S(1)} all-gather(bf16[128,64]{0,1:T(8,128)(2,1)S(1)} %copy.72), channel_id=2, replica_groups=mesh['groups'=2,'tensor'=4,'seq'=2,'load'=2] {'tensor'}, dimensions={1}, use_global_device_ids=true | all-gather | bytes 81920 | tf_op jit(solution)/shard_map/all_gather | solution.py:126
  235.0 1.2 fusion.25
  236.6 4.3 %convolution_add_fusion = f32[128,4096]{1,0:T(8,128)} fusion(bf16[128,512]{0,1:T(8,128)(2,1)S(1)} %bitcast.120, bf16[512,4096]{1,0:T(8,128)(2,1)} %all-gather.3.cloned.1.call-done, f32[128,4672]{1,0:T(8,128)S(1)} %bitcast_select_fusion.4), kind=kOutput, calls=%fused_computation.5 | convolution fusion | flops 537395200 | bytes 8519680 | tf_op jit(solution)/shard_map/dot_general | solution.py:16
  240.9 1.9 copy.82
  242.8 1.5 collective-permute-start.3
  244.3 2.6 fusion.43
  246.9 2.4 copy.97
  249.4 0.7 copy.96
  250.2 2.5 collective-permute-start.4
  252.6 4.2 %fusion.15 = (bf16[128,2048,1]{1,0,2:T(8,128)(2,1)S(1)}, bf16[128,2048,1]{1,0,2:T(8,128)(2,1)S(1)}) fusion(f32[128,2048,1]{1,0,2:T(8,128)S(1)} %copy.97, f32[128,2048,1]{1,0,2:T(8,128)S(1)} %copy.96, f32[2048]{0:T(1024)S(1)} %fusion.35, f32[128]{0:T(128)S(1)} %copy-done.7), kind=kLoop, calls=%fused_computation.24 | loop fusion | flops 2359296 | bytes 3154432 | tf_op jit(solution)/shard_map/convert
  256.9 0.8 copy.85
  257.7 3.8 %collective-permute-done.4 = bf16[128,1024]{1,0:T(8,128)(2,1)S(1)} collective-permute-done((bf16[128,1024]{1,0:T(8,128)(2,1)S(1)}, bf16[128,1024]{1,0:T(8,128)(2,1)S(1)}, u32[]{:S(2)}, u32[]{:S(2)}) %collective-permute-start.4) | collective-permute-done | bytes 262176 | tf_op jit(solution)/shard_map/ppermute | solution.py:145
  262.3 6.5 %all_gather.18 = bf16[512,4,128]{2,0,1:T(8,128)(2,1)S(1)} all-gather(bf16[128,4,128]{2,0,1:T(8,128)(2,1)S(1)} %pad_maximum_fusion.3), channel_id=1, replica_groups=mesh['groups'=2,'tensor'=4,'seq'=2,'load'=2] {'seq','load'}, dimensions={0}, use_global_device_ids=true | all-gather | bytes 655360 | tf_op jit(solution)/shard_map/all_gather | solution.py:163
  268.8 5.1 %fusion.46 = (f32[2,16,128]{2,1,0:T(8,128)S(1)}, bf16[2,16,128,512]{2,3,1,0:T(8,128)(2,1)}) fusion(pred[128,512]{0,1:T(8,128)(4,1)S(1)} %compare_and_fusion, bf16[128,2,16,128]{0,3,2,1:T(8,128)(2,1)S(1)} %bitcast.114, bf16[512,4,128]{2,0,1:T(8,128)(2,1)S(1)} %all_gather.18), kind=kOutput, calls=%fused_computation.136 | convolution fusion | flops 549454336 | bytes 5652480 | tf_op jit(solution)/shard_map/sub | solution.py:180
  273.9 4.1 %fusion.7 = bf16[128,2,16,128]{3,0,2,1:T(8,128)(2,1)S(1)} fusion(bf16[2,16,128,512]{2,3,1,0:T(8,128)(2,1)} %get-tuple-element.34, f32[128,2,16]{0,2,1:T(8,128)S(1)} %bitcast.138, bf16[512,4,128]{2,0,1:T(8,128)(2,1)S(1)} %all_gather.18), kind=kOutput, calls=%fused_computation.14 | convolution fusion | flops 537919488 | bytes 5521408 | tf_op jit(solution)/shard_map/ghqk,kgd->ghqd/dot_general | solution.py:182
  278.0 0.7 copy.88
  279.2 18.4 %all_to_all.5 = bf16[4,1,32,4608]{3,2,1,0:T(8,128)(2,1)S(1)} all-to-all(bf16[4,1,32,4608]{3,2,1,0:T(8,128)(2,1)S(1)} %maximum_bitcast_fusion), channel_id=1, replica_groups=mesh['groups'=2,'tensor'=4,'seq'=2,'load'=2] {'seq','load'}, dimensions={0} | all-to-all | bytes 2359296 | tf_op jit(solution)/shard_map/all_to_all | solution.py:192
  297.7 1.1 slice.70
  298.8 0.7 slice.71
  (106 shorter events, 8.7 us)
Async XLA Ops:
  8.0 19.5 %copy-start = (bf16[4096,128]{1,0:T(8,128)(2,1)S(1)}, bf16[4096,128]{1,0:T(8,128)(2,1)}, u32[]{:S(2)}) copy-start(bf16[4096,128]{1,0:T(8,128)(2,1)} %param.14) | copy-start | bytes 3145732
  8.0 180.5 %reduce-scatter.5.cloned.1.call-start = ((), (), s32[]{:S(2)}) async-start(), calls=%async_computation.5 | async-start | bytes 3031040 | tf_op jit(solution)/shard_map/reduce_scatter | solution.py:111
  9.9 16.9 %copy-start.2 = (bf16[4096,512]{1,0:T(8,128)(2,1)S(1)}, bf16[4096,512]{1,0:T(8,128)(2,1)}, u32[]{:S(2)}) copy-start(bf16[4096,512]{1,0:T(8,128)(2,1)} %param.12) | copy-start | bytes 12582916
  9.9 16.9 %copy-start.3 = (bf16[128,4096]{1,0:T(8,128)(2,1)S(1)}, bf16[128,4096]{1,0:T(8,128)(2,1)}, u32[]{:S(2)}) copy-start(bf16[128,4096]{1,0:T(8,128)(2,1)} %param.10) | copy-start | bytes 3145732
  26.7 1.4 copy-start.4
  27.5 1.1 copy-start.9
  27.6 1.1 copy-start.10
  32.7 155.9 %reduce-scatter.7.cloned.1.call-start = ((), (), s32[]{:S(2)}) async-start(), calls=%async_computation.6 | async-start | bytes 3031040 | tf_op jit(solution)/shard_map/reduce_scatter | solution.py:111
  32.7 28.3 %collective-permute-start = (bf16[128,4096]{1,0:T(8,128)(2,1)S(1)}, bf16[128,4096]{1,0:T(8,128)(2,1)S(1)}, u32[]{:S(2)}, u32[]{:S(2)}) collective-permute-start(bf16[128,4096]{1,0:T(8,128)(2,1)S(1)} %copy-done.3), channel_id=1, source_target_pairs={{0,4},{4,8},{8,12},{12,0},{1,5},{5,9},{9,13},{13,1},{2,6},{6,10},{... | collective-permute-start | bytes 3145736 | tf_op jit(solution)/shard_map/ppermute | solution.py:98
  84.4 104.1 %reduce-scatter.9.cloned.1.call-start = ((), (), s32[]{:S(2)}) async-start(), calls=%async_computation.7 | async-start | bytes 3031040 | tf_op jit(solution)/shard_map/reduce_scatter | solution.py:111
  84.5 26.4 %collective-permute-start.1 = (bf16[128,4096]{1,0:T(8,128)(2,1)S(1)}, bf16[128,4096]{1,0:T(8,128)(2,1)S(1)}, u32[]{:S(2)}, u32[]{:S(2)}) collective-permute-start(bf16[128,4096]{1,0:T(8,128)(2,1)S(1)} %collective-permute-done), channel_id=1, source_target_pairs={{0,4},{4,8},{8,12},{12,0},{1,5},{5,9},{9,13},{13,1},{2,6},{6,10},{... | collective-permute-start | bytes 3145736 | tf_op jit(solution)/shard_map/ppermute | solution.py:98
  134.3 80.0 %reduce-scatter.11.cloned.1.call-start = ((), (), s32[]{:S(2)}) async-start(), calls=%async_computation.8 | async-start | bytes 3031040 | tf_op jit(solution)/shard_map/reduce_scatter | solution.py:111
  134.4 25.2 %collective-permute-start.2 = (bf16[128,4096]{1,0:T(8,128)(2,1)S(1)}, bf16[128,4096]{1,0:T(8,128)(2,1)S(1)}, u32[]{:S(2)}, u32[]{:S(2)}) collective-permute-start(bf16[128,4096]{1,0:T(8,128)(2,1)S(1)} %collective-permute-done.1), channel_id=1, source_target_pairs={{0,4},{4,8},{8,12},{12,0},{1,5},{5,9},{9,13},{13,1},{2,6},{6,10},{... | collective-permute-start | bytes 3145736 | tf_op jit(solution)/shard_map/ppermute | solution.py:98
  183.1 1.9 copy-start.6
  183.1 53.5 %all-gather.3.cloned.1.call-start = ((), (), s32[]{:S(2)}) async-start(), calls=%async_computation.9 | async-start | bytes 6291456 | tf_op jit(solution)/shard_map/all_gather | solution.py:92
  220.4 14.6 %copy-start.7 = (f32[128]{0:T(128)S(1)}, f32[128]{0:T(128)}, u32[]{:S(2)}) copy-start(f32[128]{0:T(128)} %subtract_convert_fusion) | copy-start | bytes 1540
  240.9 1.9 copy-start.8
  242.8 7.2 %collective-permute-start.3 = (bf16[128,512]{1,0:T(8,128)(2,1)S(1)}, bf16[128,512]{1,0:T(8,128)(2,1)S(1)}, u32[]{:S(2)}, u32[]{:S(2)}) collective-permute-start(bf16[128,512]{1,0:T(8,128)(2,1)S(1)} %select_convert_fusion), channel_id=1, source_target_pairs={{0,4},{4,0},{8,12},{12,8},{1,5},{5,1},{9,13},{13,9},{2,6},{6,2},{1... | collective-permute-start | bytes 393224 | tf_op jit(solution)/shard_map/ppermute | solution.py:145
  246.9 2.4 copy-start.5
  250.2 11.4 %collective-permute-start.4 = (bf16[128,1024]{1,0:T(8,128)(2,1)S(1)}, bf16[128,1024]{1,0:T(8,128)(2,1)S(1)}, u32[]{:S(2)}, u32[]{:S(2)}) collective-permute-start(bf16[128,1024]{1,0:T(8,128)(2,1)S(1)} %maximum_select_fusion.1), channel_id=1, source_target_pairs={{0,8},{4,12},{8,0},{12,4},{1,9},{5,13},{9,1},{13,5},{2,10},{6,14},... | collective-permute-start | bytes 786440 | tf_op jit(solution)/shard_map/ppermute | solution.py:145
  279.1 20.3 %copy-start.1 = (bf16[4096,128]{1,0:T(8,128)(2,1)S(1)}, bf16[4096,128]{1,0:T(8,128)(2,1)}, u32[]{:S(2)}) copy-start(bf16[4096,128]{1,0:T(8,128)(2,1)} %param.14) | copy-start | bytes 3145732
Sparse Core Ops, SparseCore 0:
  32.8 36.1 reduce-scatter.4
  84.6 32.8 reduce-scatter.6
  134.5 31.3 reduce-scatter.8
  183.2 31.1 reduce-scatter.10
Sparse Core Ops, SparseCore 1:
  185.1 11.2 all-gather.2
